TPU v7x, 256 devices: a whole 4x4x8 slice. The times are simulated.
256 devices in a mesh: seq: 32 (over x, z), head: 8 (over y, core).
Axes of the slice: x: 4, y: 4, z: 8, core: 2. Of those that a mesh axis runs over, the one named last changes fastest.
Arguments:
- queries: bfloat16 [4, 8192, 2048], P(None, 'seq', 'head'), may hold values from -6 to 6
- keys: bfloat16 [4, 8192, 2048], P(None, 'seq', 'head'), may hold values from -6 to 6
- values: bfloat16 [4, 8192, 2048], P(None, 'seq', 'head'), may hold values from -6 to 6
- out_grad: bfloat16 [4, 8192, 2048], P(None, ('seq', 'head')), may hold values from -6 to 6
- selected: int32 [4, 32, 16, 2], P(None, None, 'head'), may hold values from 0 to 63, as said below
Outputs:
- attended: bfloat16 [4, 8192, 2048], P(None, 'seq', 'head')
- query_gradient: bfloat16 [4, 8192, 2048], P(None, 'seq', 'head')
- key_grad: bfloat16 [4, 8192, 2048], P(None, 'seq', 'head')
- value_grad: bfloat16 [4, 8192, 2048], P(None, 'seq', 'head')
Inputs may be any that keep to these rules, and one draw needn't show every extreme that they name: selected[f, s, h, j] selects for head h an earlier block of the query block that device s holds in slice f (block s // 2, 31 - s // 2, 32 + s // 2, 63 - s // 2 for f = 0, 1, 2, 3); an entry not smaller than that block's number selects nothing. Rows 2 m and 2 m + 1 are equal. Let the group of block b be r or 31 - r, whichever is smaller, with r = b mod 32. For one head and one m, the usable entries of the four query blocks lie in different groups, none of them group m.
All inputs are finite; a program needn't handle non-finite values.
Results may differ from a plain program's by a relative error of at most 0.0074.
Values may be sent and summed in bfloat16 or wider, within the bound.
No kernel may reach another device: no remote copies, remote signals or barrier semaphores. Data moves between devices by JAX's collectives and lax.ppermute only.
A program may use at most 128 MiB of HBM per device.

v0:
```python
import math

import jax
import jax.numpy as jnp
from jax import lax
from jax.sharding import Mesh, PartitionSpec as P


HD = 128


def swap_pair(value):
    return lax.ppermute(value, "sp", [(0, 1), (1, 0)])


def per_head(stored, head_count):
    slices = stored.shape[0]
    rows = stored.shape[1]
    return stored.reshape(slices, rows, head_count, HD).transpose(2, 0, 1, 3)


def merge_heads(split):
    head_count = split.shape[0]
    slices = split.shape[1]
    rows = split.shape[2]
    return split.transpose(1, 2, 0, 3).reshape(slices, rows, head_count * HD)


def layer(queries, keys, values, out_grad, selected):
    groups = lax.axis_size("sg")
    seq_count = 2 * groups
    group_id = lax.axis_index("sg")
    parity = lax.axis_index("sp")
    slices = queries.shape[0]
    half_len = queries.shape[1]
    block_len = 2 * half_len
    head_count = queries.shape[2] // HD
    logit_scale_factor = 1.0 / math.sqrt(HD)
    q_heads = per_head(queries, head_count)
    k_heads = per_head(keys, head_count)
    v_heads = per_head(values, head_count)
    grad_rows = lax.all_to_all(out_grad, "head", split_axis=2, concat_axis=1, tiled=True)
    g_heads = per_head(grad_rows, head_count)
    kv = jnp.stack([k_heads, v_heads])

    sel_g = selected[:, 0::2]
    gid = jnp.arange(groups, dtype=jnp.int32)
    query_block = jnp.stack([gid, seq_count - 1 - gid, seq_count + gid, 2 * seq_count - 1 - gid])
    usable_g = sel_g < query_block[:, :, None, None]
    mine_block = jnp.stack(
        [group_id, seq_count - 1 - group_id, seq_count + group_id, 2 * seq_count - 1 - group_id]
    )
    hits = usable_g[..., None] & (sel_g[..., None] == mine_block)
    need = jnp.any(hits, axis=(0, 3)).astype(jnp.bfloat16)
    mine_sel = lax.dynamic_index_in_dim(sel_g, group_id, 1, keepdims=False)
    mine_usable = mine_sel < mine_block[:, None, None]
    fold = mine_sel % seq_count
    src_group = jnp.where(fold >= groups, seq_count - 1 - fold, fold)
    src_group = jnp.where(mine_usable, src_group, 0)

    send = jnp.einsum(
        "ghf,chfld->gchld", need, kv, preferred_element_type=jnp.float32
    ).astype(jnp.bfloat16)
    held_half = (jnp.arange(slices, dtype=jnp.int32) + parity) % 2
    pairs_kv = kv.reshape(2, head_count, slices // 2, 2, half_len, HD)
    lead = jnp.where(parity == 0, pairs_kv[:, :, :, 0], pairs_kv[:, :, :, 1])
    mate = swap_pair(lead)

    empty_span = jnp.zeros((2, head_count, half_len, HD), jnp.bfloat16)
    own_rows = []
    for slice_id in range(slices):
        second = jnp.concatenate([mate[:, :, slice_id // 2], kv[:, :, slice_id]], axis=2)
        first = jnp.concatenate([kv[:, :, slice_id], empty_span], axis=2)
        own_rows.append(jnp.where(held_half[slice_id] == 1, second, first))
    own_kv = jnp.stack(own_rows, axis=0)

    key_pos = jnp.arange(block_len, dtype=jnp.int32)
    query_pos = held_half[:, None] * half_len + jnp.arange(half_len, dtype=jnp.int32)[None, :]
    own_vis = key_pos[None, None, :] <= query_pos[:, :, None]
    sel_vis = jnp.repeat(mine_usable, block_len, axis=2)
    topk = sel_g.shape[3]

    def attend(operands):
        q_one, k_one, v_one, g_one, vis_one = operands
        attention_logits = (
            jnp.einsum("qd,kd->qk", q_one, k_one, preferred_element_type=jnp.float32)
            * logit_scale_factor
        )
        masked = jnp.where(vis_one, attention_logits, -jnp.inf)
        row_max = jnp.max(masked, axis=-1, keepdims=True)
        exp_vals = jnp.exp(masked - row_max)
        probs = exp_vals / jnp.sum(exp_vals, axis=-1, keepdims=True)
        probability_narrow = probs.astype(jnp.bfloat16)
        attended = jnp.einsum(
            "qk,kd->qd", probability_narrow, v_one, preferred_element_type=jnp.float32
        ).astype(jnp.bfloat16)
        probability_gradient = jnp.einsum(
            "qd,kd->qk", g_one, v_one, preferred_element_type=jnp.float32
        )
        row_delta = jnp.sum(probs * probability_gradient, axis=-1, keepdims=True)
        score_gradient = (probs * (probability_gradient - row_delta)).astype(jnp.bfloat16)
        query_gradient = (
            logit_scale_factor
            * jnp.einsum("qk,kd->qd", score_gradient, k_one, preferred_element_type=jnp.float32)
        ).astype(jnp.bfloat16)
        key_terms = logit_scale_factor * jnp.einsum(
            "qk,qd->kd", score_gradient, q_one, preferred_element_type=jnp.float32
        )
        value_terms = jnp.einsum(
            "qk,qd->kd", probability_narrow, g_one, preferred_element_type=jnp.float32
        )
        return (attended, query_gradient, jnp.stack([key_terms, value_terms]))

    attended_heads = []
    query_heads = []
    outgoing = []
    owned = []
    for head in range(head_count):
        got = lax.all_to_all(send[:, :, head], "sg", split_axis=0, concat_axis=0, tiled=True)
        taken = got[src_group[:, head]]
        other = swap_pair(taken)
        sel_kv = jnp.stack([taken, other], axis=2)
        sel_kv = sel_kv.transpose(0, 3, 1, 2, 4, 5).reshape(
            slices, 2, 2 * topk * half_len, HD
        )
        every_kv = jnp.concatenate([own_kv[:, :, head], sel_kv], axis=2)
        visible = jnp.concatenate(
            [
                own_vis,
                jnp.broadcast_to(
                    sel_vis[:, head, None, :], (slices, half_len, sel_vis.shape[2])
                ),
            ],
            axis=-1,
        )
        attended, query_gradient, terms = lax.map(
            attend,
            (q_heads[head], every_kv[:, 0], every_kv[:, 1], g_heads[head], visible),
        )
        sel_terms = terms[:, :, block_len:].reshape(slices, 2, topk, 2, half_len, HD)
        mine_terms = sel_terms[:, :, :, 0]
        other_terms = sel_terms[:, :, :, 1].astype(jnp.bfloat16)
        by_pair = terms[:, :, :half_len].reshape(slices // 2, 2, 2, half_len, HD)
        trail = jnp.where(parity == 0, by_pair[:, 1], by_pair[:, 0]).astype(jnp.bfloat16)
        item_count = other_terms.size // (half_len * HD)
        both = jnp.concatenate(
            [other_terms.reshape(item_count, half_len, HD), trail.reshape(-1, half_len, HD)]
        )
        both = swap_pair(both)
        partner_terms = both[:item_count].reshape(other_terms.shape)
        mate_back = both[item_count:].reshape(trail.shape)
        summed = (mine_terms + partner_terms.astype(jnp.float32)).astype(jnp.bfloat16)
        route = (
            (src_group[None, :, head] == gid[:, None, None]) & mine_usable[None, :, head]
        ).astype(jnp.bfloat16)
        send_back = jnp.einsum(
            "gfj,fcjld->gcld", route, summed, preferred_element_type=jnp.float32
        ).astype(jnp.bfloat16)
        outgoing.append(send_back)
        rows_kept = []
        for slice_id in range(slices):
            first = terms[slice_id, :, :half_len] + mate_back[slice_id // 2].astype(jnp.float32)
            second = terms[slice_id, :, half_len:block_len]
            rows_kept.append(jnp.where(held_half[slice_id] == 0, first, second))
        owned.append(jnp.stack(rows_kept, axis=1))
        attended_heads.append(attended)
        query_heads.append(query_gradient)

    back = lax.all_to_all(jnp.stack(outgoing, axis=2), "sg", split_axis=0, concat_axis=0, tiled=True)
    gathered = jnp.einsum("ghf,gchld->chfld", need, back, preferred_element_type=jnp.float32)
    grads = (jnp.stack(owned, axis=1) + gathered).astype(jnp.bfloat16)
    return (
        merge_heads(jnp.stack(attended_heads)),
        merge_heads(jnp.stack(query_heads)),
        merge_heads(grads[0]),
        merge_heads(grads[1]),
    )


def solution(mesh):
    seq_count = mesh.shape["seq"]
    head_count = mesh.shape["head"]
    pair_mesh = Mesh(
        mesh.devices.reshape(seq_count // 2, 2, head_count), ("sg", "sp", "head")
    )
    tokens = P(None, ("sg", "sp"), "head")
    in_specs = (
        tokens,
        tokens,
        tokens,
        P(None, ("sg", "sp", "head"), None),
        P(None, None, "head", None),
    )
    out_specs = (tokens, tokens, tokens, tokens)
    return jax.shard_map(
        layer, mesh=pair_mesh, in_specs=in_specs, out_specs=out_specs, check_vma=False
    )
```

profile of v0, /device:TPU:2, one launch (start us, length us, event | category | flops | bytes accessed | tf_op | source)
XLA Modules:
  0.0 429.3 jit_solution(6398588734992555590)
XLA Ops:
  0.6 2.8 copy.324
  3.5 2.7 reshape.342
  6.1 4.6 %all-to-all-start.1 = ((bf16[8,2,16384]{2,1,0:T(2,128)(2,1)}), bf16[8,2,16384]{2,1,0:T(2,128)(2,1)}, u32[]{:S(2)}, u32[]{:S(2)}) async-start(bf16[8,2,16384]{2,1,0:T(2,128)(2,1)} %reshape.342), calls=%async_computation.1 | async-start | bytes 1048576 | tf_op jit(solution)/shard_map/all_to_all | solution.py:42
  14.5 1.9 copy.327
  16.4 4.8 %all-to-all-done.1 = bf16[8,2,16384]{2,1,0:T(2,128)(2,1)} async-done(((bf16[8,2,16384]{2,1,0:T(2,128)(2,1)}), bf16[8,2,16384]{2,1,0:T(2,128)(2,1)}, u32[]{:S(2)}, u32[]{:S(2)}) %all-to-all-start.1) | async-done | bytes 524320 | tf_op jit(solution)/shard_map/all_to_all | solution.py:42
  21.2 11.5 %all-to-all-start.2 = ((bf16[16,2,256,128]{3,2,1,0:T(8,128)(2,1)}), bf16[16,2,256,128]{3,2,1,0:T(8,128)(2,1)}, u32[]{:S(2)}, u32[]{:S(2)}) async-start(bf16[16,2,256,128]{3,2,1,0:T(8,128)(2,1)} %copy.327), calls=%async_computation.2 | async-start | bytes 4194304 | tf_op jit(solution)/shard_map/all_to_all | solution.py:119
  34.4 2.1 fusion.103
  37.9 1.9 copy.320
  41.0 43.5 %all-to-all-done.2 = bf16[16,2,256,128]{3,2,1,0:T(8,128)(2,1)} async-done(((bf16[16,2,256,128]{3,2,1,0:T(8,128)(2,1)}), bf16[16,2,256,128]{3,2,1,0:T(8,128)(2,1)}, u32[]{:S(2)}, u32[]{:S(2)}) %all-to-all-start.2) | async-done | bytes 2097184 | tf_op jit(solution)/shard_map/all_to_all | solution.py:119
  84.5 7.0 %all-to-all-start = ((bf16[16,2,256,128]{3,2,1,0:T(8,128)(2,1)}), bf16[16,2,256,128]{3,2,1,0:T(8,128)(2,1)}, u32[]{:S(2)}, u32[]{:S(2)}) async-start(bf16[16,2,256,128]{3,2,1,0:T(8,128)(2,1)} %copy.320), calls=%async_computation | async-start | bytes 4194304 | tf_op jit(solution)/shard_map/all_to_all | solution.py:119
  92.6 3.0 fusion.104
  97.1 1.9 pad_add_fusion.1
  101.6 3.6 reshape.343
  107.2 2.3 gather_fusion.1
  113.4 1.5 slice_bitcast_fusion.3
  114.9 26.6 %all-to-all-done = bf16[16,2,256,128]{3,2,1,0:T(8,128)(2,1)} async-done(((bf16[16,2,256,128]{3,2,1,0:T(8,128)(2,1)}), bf16[16,2,256,128]{3,2,1,0:T(8,128)(2,1)}, u32[]{:S(2)}, u32[]{:S(2)}) %all-to-all-start) | async-done | bytes 2097184 | tf_op jit(solution)/shard_map/all_to_all | solution.py:119
  141.5 2.3 gather_fusion
  144.5 14.3 %collective-permute-done.2 = bf16[4,2,2,256,128]{4,3,2,1,0:T(8,128)(2,1)} collective-permute-done((bf16[4,2,2,256,128]{4,3,2,1,0:T(8,128)(2,1)S(1)}, bf16[4,2,2,256,128]{4,3,2,1,0:T(8,128)(2,1)}, u32[]{:S(2)}, u32[]{:S(2)}) %collective-permute-start.2) | collective-permute-done | bytes 1048608 | tf_op jit(solution)/shard_map/ppermute | solution.py:13
  158.8 1.4 maximum_bitcast_fusion.3
  161.5 1.4 fusion.89
  163.7 3.2 broadcast.193.clone
  166.8 27.3 %while.29 = (s32[]{:T(128)}, bf16[4,256,128]{2,1,0:T(8,128)(2,1)}, bf16[4,256,128]{2,1,0:T(8,128)(2,1)S(1)}, f32[4,2,1536,128]{3,2,1,0:T(8,128)}, pred[4,256,153...) while((s32[]{:T(128)}, bf16[4,256,128]{2,1,0:T(8,128)(2,1)}, ...), condition=%wide.region_10.11_spmd, body=%wide.region_6.10_spmd.sunk | while | flops 612531456 | bytes 29378224 | solution.py:136
  166.8 1.6 fusion.200
  173.7 1.6 fusion.200
  180.5 1.6 fusion.200
  187.3 1.6 fusion.200
  194.1 1.4 slice.280
  195.5 4.4 %slice.278 = f32[4,2,1024,128]{3,2,1,0:T(8,128)} slice(f32[4,2,1536,128]{3,2,1,0:T(8,128)} %get-tuple-element.107), slice={[0:4], [0:2], [512:1536], [0:128]} | slice | bytes 8388608 | tf_op jit(solution)/shard_map/slice | solution.py:140
  200.0 1.4 maximum_bitcast_fusion.2
  204.8 3.2 broadcast.193.clone.1
  207.9 29.0 %while.28 = (s32[]{:T(128)}, bf16[4,256,128]{2,1,0:T(8,128)(2,1)S(1)}, bf16[4,256,128]{2,1,0:T(8,128)(2,1)}, f32[4,2,1536,128]{3,2,1,0:T(8,128)}, pred[4,256,153...) while((s32[]{:T(128)}, ...), condition=%wide.region_5.6_spmd, body=%wide.region_1.5_spmd.sunk | while | flops 612531456 | bytes 29378224 | solution.py:136
  207.9 1.6 fusion.186
  215.2 1.6 fusion.186
  222.4 1.6 fusion.186
  229.6 1.6 fusion.186
  238.3 2.6 slice.263
  242.2 2.3 collective-permute-start.4
  245.6 28.5 %collective-permute-done.4 = bf16[20,256,128]{2,1,0:T(8,128)(2,1)S(1)} collective-permute-done((bf16[20,256,128]{2,1,0:T(8,128)(2,1)S(1)}, bf16[20,256,128]{2,1,0:T(8,128)(2,1)S(1)}, u32[]{:S(2)}, u32[]{:S(2)}) %collective-permute-start.4) | collective-permute-done | bytes 1310752 | tf_op jit(solution)/shard_map/ppermute | solution.py:13
  274.4 25.2 %collective-permute-done.3 = bf16[20,256,128]{2,1,0:T(8,128)(2,1)S(1)} collective-permute-done((bf16[20,256,128]{2,1,0:T(8,128)(2,1)S(1)}, bf16[20,256,128]{2,1,0:T(8,128)(2,1)S(1)}, u32[]{:S(2)}, u32[]{:S(2)}) %collective-permute-start.3) | collective-permute-done | bytes 1310752 | tf_op jit(solution)/shard_map/ppermute | solution.py:13
  300.0 3.6 fusion.84
  303.6 3.7 fusion.83
  307.6 3.1 copy.352
  310.7 9.8 %all-to-all-start.3 = ((bf16[16,2,2,256,128]{4,3,1,2,0:T(8,128)(2,1)}), bf16[16,2,2,256,128]{4,3,1,2,0:T(8,128)(2,1)}, u32[]{:S(2)}, u32[]{:S(2)}) async-start(bf16[16,2,2,256,128]{4,3,1,2,0:T(8,128)(2,1)} %copy.352), calls=%async_computation.3 | async-start | bytes 8388608 | tf_op jit(solution)/shard_map/all_to_all | solution.py:169
  323.0 1.8 copy_bitcast_fusion.3
  325.7 1.6 fusion.113
  328.1 1.6 fusion.120
  330.7 90.4 %all-to-all-done.3 = bf16[16,2,2,256,128]{4,3,1,2,0:T(8,128)(2,1)} async-done(((bf16[16,2,2,256,128]{4,3,1,2,0:T(8,128)(2,1)}), bf16[16,2,2,256,128]{4,3,1,2,0:T(8,128)(2,1)}, u32[]{:S(2)}, u32[]{:S(2)}) %all-to-all-start.3) | async-done | bytes 4194336 | tf_op jit(solution)/shard_map/all_to_all | solution.py:169
  421.1 4.9 %fusion.76 = bf16[2,2,4,256,128]{4,2,3,0,1:T(4,128)(2,1)S(1)} fusion(f32[2,1,4,256,128]{4,2,3,0,1:T(4,128)S(1)} %maximum_bitcast_fusion.5, f32[2,1,4,256,128]{4,2,3,0,1:T(4,128)S(1)} %copy.343, bf16[16,2,2,256,128]{4,3,1,2,0:T(8,128)(2,1)} %all-to-all-done.3, pred[16,2,4]{0,2,1:T(4,128)(4,1)S(1)} %copy-done.20), kind=kOutput, calls=%fused_computation.110 | convolution fusion | flops 18350080 | bytes 7340160 | tf_op jit(solution)/shard_map/ghf,gchld->chfld/dot_general | solution.py:170
  (217 shorter events, 75.4 us)
Async XLA Ops:
  3.4 7.3 %copy-start.18 = (s32[4,32,2,2]{1,3,2,0:T(2,128)S(1)}, s32[4,32,2,2]{1,3,2,0:T(2,128)}, u32[]{:S(2)}) copy-start(s32[4,32,2,2]{1,3,2,0:T(2,128)} %param.13) | copy-start | bytes 6148
  3.5 7.8 %copy-start.13 = (bf16[4,256,256]{2,1,0:T(8,128)(2,1)S(1)}, bf16[4,256,256]{2,1,0:T(8,128)(2,1)}, u32[]{:S(2)}) copy-start(bf16[4,256,256]{2,1,0:T(8,128)(2,1)} %param.10) | copy-start | bytes 1572868
  6.1 5.6 %copy-start.14 = (bf16[4,256,256]{2,1,0:T(8,128)(2,1)S(1)}, bf16[4,256,256]{2,1,0:T(8,128)(2,1)}, u32[]{:S(2)}) copy-start(bf16[4,256,256]{2,1,0:T(8,128)(2,1)} %param.11) | copy-start | bytes 1572868
  6.1 15.0 %all-to-all-start.1 = ((bf16[8,2,16384]{2,1,0:T(2,128)(2,1)}), bf16[8,2,16384]{2,1,0:T(2,128)(2,1)}, u32[]{:S(2)}, u32[]{:S(2)}) async-start(bf16[8,2,16384]{2,1,0:T(2,128)(2,1)} %reshape.342), calls=%async_computation.1 | async-start | bytes 1048576 | tf_op jit(solution)/shard_map/all_to_all | solution.py:42
  12.5 1.3 copy-start.19
  21.2 63.3 %all-to-all-start.2 = ((bf16[16,2,256,128]{3,2,1,0:T(8,128)(2,1)}), bf16[16,2,256,128]{3,2,1,0:T(8,128)(2,1)}, u32[]{:S(2)}, u32[]{:S(2)}) async-start(bf16[16,2,256,128]{3,2,1,0:T(8,128)(2,1)} %copy.327), calls=%async_computation.2 | async-start | bytes 4194304 | tf_op jit(solution)/shard_map/all_to_all | solution.py:119
  36.4 75.1 %collective-permute-start = (bf16[2,2,2,256,128]{4,3,2,1,0:T(8,128)(2,1)}, bf16[2,2,2,256,128]{4,3,2,1,0:T(8,128)(2,1)}, u32[]{:S(2)}, u32[]{:S(2)}) collective-permute-start(bf16[2,2,2,256,128]{4,3,2,1,0:T(8,128)(2,1)} %fusion.103), channel_id=1, source_target_pairs={{0,8},{8,0},{1,9},{9,1},{2,10},{10,2},{3,11},{11,3},{4,12},{12,4},... | collective-permute-start | bytes 1572872 | tf_op jit(solution)/shard_map/ppermute | solution.py:13
  41.0 50.7 %copy-start.15 = (bf16[4,256,256]{2,1,0:T(8,128)(2,1)S(1)}, bf16[4,256,256]{2,1,0:T(8,128)(2,1)}, u32[]{:S(2)}) copy-start(bf16[4,256,256]{2,1,0:T(8,128)(2,1)} %param.9) | copy-start | bytes 1572868
  84.5 57.1 %all-to-all-start = ((bf16[16,2,256,128]{3,2,1,0:T(8,128)(2,1)}), bf16[16,2,256,128]{3,2,1,0:T(8,128)(2,1)}, u32[]{:S(2)}, u32[]{:S(2)}) async-start(bf16[16,2,256,128]{3,2,1,0:T(8,128)(2,1)} %copy.320), calls=%async_computation | async-start | bytes 4194304 | tf_op jit(solution)/shard_map/all_to_all | solution.py:119
  109.6 3.0 copy-start.6
  109.6 3.0 copy-start.7
  109.6 49.2 %collective-permute-start.2 = (bf16[4,2,2,256,128]{4,3,2,1,0:T(8,128)(2,1)S(1)}, bf16[4,2,2,256,128]{4,3,2,1,0:T(8,128)(2,1)}, u32[]{:S(2)}, u32[]{:S(2)}) collective-permute-start(bf16[4,2,2,256,128]{4,3,2,1,0:T(8,128)(2,1)S(1)} %bitcast.460), channel_id=1, source_target_pairs={{0,8},{8,0},{1,9},{9,1},{2,10},{10,2},{3,11},{11,3},{4,12},{12,4},... | collective-permute-start | bytes 3145736 | tf_op jit(solution)/shard_map/ppermute | solution.py:13
  143.9 56.1 %collective-permute-start.1 = (bf16[4,2,2,256,128]{4,3,2,1,0:T(8,128)(2,1)S(1)}, bf16[4,2,2,256,128]{4,3,2,1,0:T(8,128)(2,1)}, u32[]{:S(2)}, u32[]{:S(2)}) collective-permute-start(bf16[4,2,2,256,128]{4,3,2,1,0:T(8,128)(2,1)S(1)} %bitcast.458), channel_id=1, source_target_pairs={{0,8},{8,0},{1,9},{9,1},{2,10},{10,2},{3,11},{11,3},{4,12},{12,4},... | collective-permute-start | bytes 3145736 | tf_op jit(solution)/shard_map/ppermute | solution.py:13
  160.2 1.2 copy-start.2
  163.7 3.2 copy-start.3
  166.8 2.0 copy-start.5
  168.8 1.1 copy-start.17
  173.7 2.0 copy-start.5
  175.7 1.1 copy-start.17
  180.5 2.0 copy-start.5
  182.5 1.1 copy-start.17
  187.3 2.0 copy-start.5
  189.3 1.1 copy-start.17
  194.1 5.8 %copy-start.11 = (bf16[4,256,128]{2,1,0:T(8,128)(2,1)}, bf16[4,256,128]{2,1,0:T(8,128)(2,1)S(1)}, u32[]{:S(2)}) copy-start(bf16[4,256,128]{2,1,0:T(8,128)(2,1)S(1)} %get-tuple-element.105) | copy-start | bytes 786436
  201.4 1.2 copy-start.1
  207.9 2.0 copy-start.4
  209.9 1.0 copy-start.16
  215.2 2.0 copy-start.4
  217.2 1.0 copy-start.16
  222.4 2.0 copy-start.4
  224.4 1.0 copy-start.16
  229.6 2.0 copy-start.4
  231.6 1.0 copy-start.16
  236.9 4.1 copy-start.8
  238.3 3.5 copy-start
  242.2 31.9 %collective-permute-start.4 = (bf16[20,256,128]{2,1,0:T(8,128)(2,1)S(1)}, bf16[20,256,128]{2,1,0:T(8,128)(2,1)S(1)}, u32[]{:S(2)}, u32[]{:S(2)}) collective-permute-start(bf16[20,256,128]{2,1,0:T(8,128)(2,1)S(1)} %pad_maximum_fusion.5), channel_id=1, source_target_pairs={{0,8},{8,0},{1,9},{9,1},{2,10},{10,2},{3,11},{11,3},{4,12},{12,4},... | collective-permute-start | bytes 3932168 | tf_op jit(solution)/shard_map/ppermute | solution.py:13
  244.9 54.8 %collective-permute-start.3 = (bf16[20,256,128]{2,1,0:T(8,128)(2,1)S(1)}, bf16[20,256,128]{2,1,0:T(8,128)(2,1)S(1)}, u32[]{:S(2)}, u32[]{:S(2)}) collective-permute-start(bf16[20,256,128]{2,1,0:T(8,128)(2,1)S(1)} %pad_maximum_fusion.4), channel_id=1, source_target_pairs={{0,8},{8,0},{1,9},{9,1},{2,10},{10,2},{3,11},{11,3},{4,12},{12,4},... | collective-permute-start | bytes 3932168 | tf_op jit(solution)/shard_map/ppermute | solution.py:13
  310.7 12.3 %copy-start.9 = (bf16[4,256,128]{2,1,0:T(8,128)(2,1)S(1)}, bf16[4,256,128]{2,1,0:T(8,128)(2,1)}, u32[]{:S(2)}) copy-start(bf16[4,256,128]{2,1,0:T(8,128)(2,1)} %copy-done.8) | copy-start | bytes 786436
  310.7 14.1 %copy-start.10 = (bf16[4,256,128]{2,1,0:T(8,128)(2,1)S(1)}, bf16[4,256,128]{2,1,0:T(8,128)(2,1)}, u32[]{:S(2)}) copy-start(bf16[4,256,128]{2,1,0:T(8,128)(2,1)} %get-tuple-element.104) | copy-start | bytes 786436
  310.7 14.1 %copy-start.12 = (bf16[4,256,128]{2,1,0:T(8,128)(2,1)S(1)}, bf16[4,256,128]{2,1,0:T(8,128)(2,1)}, u32[]{:S(2)}) copy-start(bf16[4,256,128]{2,1,0:T(8,128)(2,1)} %copy-done.11) | copy-start | bytes 786436
  310.7 110.4 %all-to-all-start.3 = ((bf16[16,2,2,256,128]{4,3,1,2,0:T(8,128)(2,1)}), bf16[16,2,2,256,128]{4,3,1,2,0:T(8,128)(2,1)}, u32[]{:S(2)}, u32[]{:S(2)}) async-start(bf16[16,2,2,256,128]{4,3,1,2,0:T(8,128)(2,1)} %copy.352), calls=%async_computation.3 | async-start | bytes 8388608 | tf_op jit(solution)/shard_map/all_to_all | solution.py:169
  329.7 91.4 %copy-start.20 = (pred[16,2,4]{0,2,1:T(4,128)(4,1)S(1)}, pred[16,2,4]{0,2,1:T(4,128)(4,1)}, u32[]{:S(2)}) copy-start(pred[16,2,4]{0,2,1:T(4,128)(4,1)} %copy-done.19) | copy-start | bytes 388
where the time goes:
time: 436 us; the launch traced here: 429 us
  waiting for transfers between devices  233 us (53%)
  local copies, waits for them, and re-layouts  61.1 us (14%)
  matrix products  50.8 us (12%)
  other arithmetic  39 us (9%)
  starting transfers between devices  38.1 us (9%)
  between operations  6.55 us (2%)
    all_to_all x1, waiting for transfers between devices, layer(): lax.all_to_all(jnp.stack(outgoing, axis=2), 'sg', split_axis=0, concat_ax...  90.4 us
    all_to_all x2, waiting for transfers between devices, layer(): lax.all_to_all(send[:, :, head], 'sg', split_axis=0, concat_axis=0, tiled...  70.1 us
    ppermute x5, waiting for transfers between devices, swap_pair(): return lax.ppermute(value, 'sp', [(0, 1), (1, 0)])  68.1 us
    all_to_all x2, starting transfers between devices, layer(): lax.all_to_all(send[:, :, head], 'sg', split_axis=0, concat_axis=0, tiled...  18.5 us
    unnamed x45, local copies, waits for them, and re-layouts  15.7 us
    dot_general x8, matrix products, attend(): jnp.einsum('qd,kd->qk', q_one, k_one, preferred_element_type=jnp.float32)  13 us
    dynamic_update_slice x8, other arithmetic, layer(): lax.map(attend, (q_heads[head], every_kv[:, 0], every_kv[:, 1], g_heads[h...  10.3 us
    all_to_all x1, starting transfers between devices, layer(): lax.all_to_all(jnp.stack(outgoing, axis=2), 'sg', split_axis=0, concat_ax...  9.78 us
  transfers between devices with their start and end apart: 9, of which 7 were waited for; matrix products, arithmetic and copies ran while one was open for 19% of the time, Pallas kernels for 0%

commit v1 on v0

--- a/solution.py
+++ b/solution.py
@@ -64,15 +64,17 @@
     held_half = (jnp.arange(slices, dtype=jnp.int32) + parity) % 2
     pairs_kv = kv.reshape(2, head_count, slices // 2, 2, half_len, HD)
     lead = jnp.where(parity == 0, pairs_kv[:, :, :, 0], pairs_kv[:, :, :, 1])
-    mate = swap_pair(lead)
-
-    empty_span = jnp.zeros((2, head_count, half_len, HD), jnp.bfloat16)
-    own_rows = []
-    for slice_id in range(slices):
-        second = jnp.concatenate([mate[:, :, slice_id // 2], kv[:, :, slice_id]], axis=2)
-        first = jnp.concatenate([kv[:, :, slice_id], empty_span], axis=2)
-        own_rows.append(jnp.where(held_half[slice_id] == 1, second, first))
-    own_kv = jnp.stack(own_rows, axis=0)
+
+    def own_keys(mate):
+
+        empty_span = jnp.zeros((2, head_count, half_len, HD), jnp.bfloat16)
+        own_rows = []
+        for slice_id in range(slices):
+            second = jnp.concatenate([mate[:, :, slice_id // 2], kv[:, :, slice_id]], axis=2)
+            first = jnp.concatenate([kv[:, :, slice_id], empty_span], axis=2)
+            own_rows.append(jnp.where(held_half[slice_id] == 1, second, first))
+        own_kv = jnp.stack(own_rows, axis=0)
+        return own_kv
 
     key_pos = jnp.arange(block_len, dtype=jnp.int32)
     query_pos = held_half[:, None] * half_len + jnp.arange(half_len, dtype=jnp.int32)[None, :]
@@ -118,7 +120,16 @@
     for head in range(head_count):
         got = lax.all_to_all(send[:, :, head], "sg", split_axis=0, concat_axis=0, tiled=True)
         taken = got[src_group[:, head]]
-        other = swap_pair(taken)
+        if head == 0:
+            span_count = taken.size // (half_len * HD)
+            sent = jnp.concatenate(
+                [taken.reshape(span_count, half_len, HD), lead.reshape(-1, half_len, HD)]
+            )
+            sent = swap_pair(sent)
+            other = sent[:span_count].reshape(taken.shape)
+            own_kv = own_keys(sent[span_count:].reshape(lead.shape))
+        else:
+            other = swap_pair(taken)
         sel_kv = jnp.stack([taken, other], axis=2)
         sel_kv = sel_kv.transpose(0, 3, 1, 2, 4, 5).reshape(
             slices, 2, 2 * topk * half_len, HD

time: 436 us -> 458 us (1.050)
  the two profiles are of different devices: /device:TPU:2 before, /device:TPU:18 now
where the time goes in v1:
time: 458 us; the launch traced here: 449 us
  waiting for transfers between devices  256 us (56%)
  local copies, waits for them, and re-layouts  65 us (14%)
  matrix products  48.4 us (11%)
  other arithmetic  38.2 us (8%)
  starting transfers between devices  34.9 us (8%)
  between operations  6.48 us (1%)
    all_to_all x1, waiting for transfers between devices, layer(): lax.all_to_all(jnp.stack(outgoing, axis=2), 'sg', split_axis=0, concat_ax...  92.1 us
    ppermute x4, waiting for transfers between devices, swap_pair(): return lax.ppermute(value, 'sp', [(0, 1), (1, 0)])  84.3 us
    all_to_all x2, waiting for transfers between devices, layer(): lax.all_to_all(send[:, :, head], 'sg', split_axis=0, concat_axis=0, tiled...  79.4 us
    unnamed x44, local copies, waits for them, and re-layouts  16.4 us
    all_to_all x2, starting transfers between devices, layer(): lax.all_to_all(send[:, :, head], 'sg', split_axis=0, concat_axis=0, tiled...  16.3 us
    dot_general x8, matrix products, attend(): jnp.einsum('qd,kd->qk', q_one, k_one, preferred_element_type=jnp.float32)  13 us
    dynamic_update_slice x8, other arithmetic, layer(): lax.map(attend, (q_heads[head], every_kv[:, 0], every_kv[:, 1], g_heads[h...  10.3 us
  transfers between devices with their start and end apart: 8, of which 6 were waited for; matrix products, arithmetic and copies ran while one was open for 10% of the time, Pallas kernels for 0%

profile of v1, /device:TPU:18, one launch (start us, length us, event | category | flops | bytes accessed | tf_op | source)
XLA Modules:
  0.0 449.4 jit_solution(12918994991277301953)
XLA Ops:
  0.7 1.7 slice.239
  6.7 1.9 copy.308
  8.6 11.5 %all-to-all-start = ((bf16[16,2,256,128]{3,2,1,0:T(8,128)(2,1)}), bf16[16,2,256,128]{3,2,1,0:T(8,128)(2,1)}, u32[]{:S(2)}, u32[]{:S(2)}) async-start(bf16[16,2,256,128]{3,2,1,0:T(8,128)(2,1)} %copy.308), calls=%async_computation | async-start | bytes 4194304 | tf_op jit(solution)/shard_map/all_to_all | solution.py:121
  20.3 1.9 copy.321
  22.2 48.4 %all-to-all-done = bf16[16,2,256,128]{3,2,1,0:T(8,128)(2,1)} async-done(((bf16[16,2,256,128]{3,2,1,0:T(8,128)(2,1)}), bf16[16,2,256,128]{3,2,1,0:T(8,128)(2,1)}, u32[]{:S(2)}, u32[]{:S(2)}) %all-to-all-start) | async-done | bytes 2097184 | tf_op jit(solution)/shard_map/all_to_all | solution.py:121
  70.6 4.8 %all-to-all-start.2 = ((bf16[16,2,256,128]{3,2,1,0:T(8,128)(2,1)}), bf16[16,2,256,128]{3,2,1,0:T(8,128)(2,1)}, u32[]{:S(2)}, u32[]{:S(2)}) async-start(bf16[16,2,256,128]{3,2,1,0:T(8,128)(2,1)} %copy.321), calls=%async_computation.2 | async-start | bytes 4194304 | tf_op jit(solution)/shard_map/all_to_all | solution.py:121
  76.7 3.8 fusion.101
  81.0 2.0 pad_add_fusion.1
  83.0 2.3 gather_fusion
  86.7 2.2 collective-permute-start
  88.9 2.8 copy.318
  91.7 2.7 reshape.354
  94.4 2.1 copy_bitcast_fusion.8
  96.4 31.0 %all-to-all-done.2 = bf16[16,2,256,128]{3,2,1,0:T(8,128)(2,1)} async-done(((bf16[16,2,256,128]{3,2,1,0:T(8,128)(2,1)}), bf16[16,2,256,128]{3,2,1,0:T(8,128)(2,1)}, u32[]{:S(2)}, u32[]{:S(2)}) %all-to-all-start.2) | async-done | bytes 2097184 | tf_op jit(solution)/shard_map/all_to_all | solution.py:121
  127.5 4.8 %all-to-all-start.1 = ((bf16[8,2,16384]{2,1,0:T(2,128)(2,1)}), bf16[8,2,16384]{2,1,0:T(2,128)(2,1)}, u32[]{:S(2)}, u32[]{:S(2)}) async-start(bf16[8,2,16384]{2,1,0:T(2,128)(2,1)} %reshape.354), calls=%async_computation.1 | async-start | bytes 1048576 | tf_op jit(solution)/shard_map/all_to_all | solution.py:42
  132.3 3.2 gather_fusion.1
  141.0 3.6 reshape.355
  144.6 2.2 copy.319
  149.6 29.2 %collective-permute-done.1 = bf16[4,2,2,256,128]{4,3,2,1,0:T(8,128)(2,1)} collective-permute-done((bf16[4,2,2,256,128]{4,3,2,1,0:T(8,128)(2,1)}, bf16[4,2,2,256,128]{4,3,2,1,0:T(8,128)(2,1)}, u32[]{:S(2)}, u32[]{:S(2)}) %collective-permute-start.1) | collective-permute-done | bytes 1048608 | tf_op jit(solution)/shard_map/ppermute | solution.py:13
  178.8 1.7 maximum_bitcast_fusion.3
  184.5 1.4 fusion.89
  186.7 3.2 broadcast.194.clone
  189.9 27.3 %while.29 = (s32[]{:T(128)}, bf16[4,256,128]{2,1,0:T(8,128)(2,1)}, bf16[4,256,128]{2,1,0:T(8,128)(2,1)S(1)}, f32[4,2,1536,128]{3,2,1,0:T(8,128)}, pred[4,256,153...) while((s32[]{:T(128)}, bf16[4,256,128]{2,1,0:T(8,128)(2,1)}, ...), condition=%wide.region_10.11_spmd, body=%wide.region_6.10_spmd.sunk | while | flops 612531456 | bytes 29378224 | solution.py:147
  189.9 1.6 fusion.196
  196.7 1.6 fusion.196
  203.5 1.6 fusion.196
  210.3 1.6 fusion.196
  217.2 1.4 slice.288
  218.6 4.4 slice.286
  227.2 3.1 broadcast.194.clone.1
  230.4 25.0 %while.28 = (s32[]{:T(128)}, bf16[4,256,128]{2,1,0:T(8,128)(2,1)S(1)}, bf16[4,256,128]{2,1,0:T(8,128)(2,1)S(1)}, f32[4,2,1536,128]{3,2,1,0:T(8,128)}, pred[4,256...) while((s32[]{:T(128)}, ...), condition=%wide.region_5.6_spmd, body=%wide.region_1.5_spmd.sunk | while | flops 612531456 | bytes 28329620 | solution.py:147
  230.5 1.6 fusion.182
  236.8 1.6 fusion.182
  243.0 1.6 fusion.182
  249.1 1.6 fusion.182
  256.7 2.6 slice.271
  261.3 1.9 collective-permute-start.2
  263.6 28.7 %collective-permute-done.3 = bf16[20,256,128]{2,1,0:T(8,128)(2,1)S(1)} collective-permute-done((bf16[20,256,128]{2,1,0:T(8,128)(2,1)S(1)}, bf16[20,256,128]{2,1,0:T(8,128)(2,1)S(1)}, u32[]{:S(2)}, u32[]{:S(2)}) %collective-permute-start.3) | collective-permute-done | bytes 1310752 | tf_op jit(solution)/shard_map/ppermute | solution.py:13
  292.6 26.3 %collective-permute-done.2 = bf16[20,256,128]{2,1,0:T(8,128)(2,1)S(1)} collective-permute-done((bf16[20,256,128]{2,1,0:T(8,128)(2,1)S(1)}, bf16[20,256,128]{2,1,0:T(8,128)(2,1)S(1)}, u32[]{:S(2)}, u32[]{:S(2)}) %collective-permute-start.2) | collective-permute-done | bytes 1310752 | tf_op jit(solution)/shard_map/ppermute | solution.py:13
  319.2 3.6 fusion.84
  322.9 3.7 fusion.83
  326.9 3.1 copy.346
  330.0 8.9 %all-to-all-start.3 = ((bf16[16,2,2,256,128]{4,3,1,2,0:T(8,128)(2,1)}), bf16[16,2,2,256,128]{4,3,1,2,0:T(8,128)(2,1)}, u32[]{:S(2)}, u32[]{:S(2)}) async-start(bf16[16,2,2,256,128]{4,3,1,2,0:T(8,128)(2,1)} %copy.346), calls=%async_computation.3 | async-start | bytes 8388608 | tf_op jit(solution)/shard_map/all_to_all | solution.py:180
  341.4 1.8 copy_bitcast_fusion.3
  344.1 1.6 fusion.110
  346.5 1.6 fusion.117
  349.1 92.1 %all-to-all-done.3 = bf16[16,2,2,256,128]{4,3,1,2,0:T(8,128)(2,1)} async-done(((bf16[16,2,2,256,128]{4,3,1,2,0:T(8,128)(2,1)}), bf16[16,2,2,256,128]{4,3,1,2,0:T(8,128)(2,1)}, u32[]{:S(2)}, u32[]{:S(2)}) %all-to-all-start.3) | async-done | bytes 4194336 | tf_op jit(solution)/shard_map/all_to_all | solution.py:180
  441.2 4.9 %fusion.76 = bf16[2,2,4,256,128]{4,2,3,0,1:T(4,128)(2,1)S(1)} fusion(f32[2,1,4,256,128]{4,2,3,0,1:T(4,128)S(1)} %maximum_bitcast_fusion.5, f32[2,1,4,256,128]{4,2,3,0,1:T(4,128)S(1)} %copy.337, bf16[16,2,2,256,128]{4,3,1,2,0:T(8,128)(2,1)} %all-to-all-done.3, pred[16,2,4]{0,2,1:T(4,128)(4,1)S(1)} %copy-done.18), kind=kOutput, calls=%fused_computation.110 | convolution fusion | flops 18350080 | bytes 7340160 | tf_op jit(solution)/shard_map/ghf,gchld->chfld/dot_general | solution.py:181
  (208 shorter events, 70.9 us)
Async XLA Ops:
  0.6 3.3 copy-start.13
  4.7 1.3 copy-start.17
  8.6 62.0 %all-to-all-start = ((bf16[16,2,256,128]{3,2,1,0:T(8,128)(2,1)}), bf16[16,2,256,128]{3,2,1,0:T(8,128)(2,1)}, u32[]{:S(2)}, u32[]{:S(2)}) async-start(bf16[16,2,256,128]{3,2,1,0:T(8,128)(2,1)} %copy.308), calls=%async_computation | async-start | bytes 4194304 | tf_op jit(solution)/shard_map/all_to_all | solution.py:121
  70.6 56.9 %all-to-all-start.2 = ((bf16[16,2,256,128]{3,2,1,0:T(8,128)(2,1)}), bf16[16,2,256,128]{3,2,1,0:T(8,128)(2,1)}, u32[]{:S(2)}, u32[]{:S(2)}) async-start(bf16[16,2,256,128]{3,2,1,0:T(8,128)(2,1)} %copy.321), calls=%async_computation.2 | async-start | bytes 4194304 | tf_op jit(solution)/shard_map/all_to_all | solution.py:121
  86.7 94.1 %collective-permute-start = (bf16[24,256,128]{2,1,0:T(8,128)(2,1)}, bf16[24,256,128]{2,1,0:T(8,128)(2,1)}, u32[]{:S(2)}, u32[]{:S(2)}) collective-permute-start(bf16[24,256,128]{2,1,0:T(8,128)(2,1)} %pad_maximum_fusion.4), channel_id=1, source_target_pairs={{0,8},{8,0},{1,9},{9,1},{2,10},{10,2},{3,11},{11,3},{4,12},{12,4},... | collective-permute-start | bytes 4718600 | tf_op jit(solution)/shard_map/ppermute | solution.py:13
  96.4 42.7 %copy-start.14 = (bf16[4,256,256]{2,1,0:T(8,128)(2,1)S(1)}, bf16[4,256,256]{2,1,0:T(8,128)(2,1)}, u32[]{:S(2)}) copy-start(bf16[4,256,256]{2,1,0:T(8,128)(2,1)} %param.9) | copy-start | bytes 1572868
  127.5 13.5 %all-to-all-start.1 = ((bf16[8,2,16384]{2,1,0:T(2,128)(2,1)}), bf16[8,2,16384]{2,1,0:T(2,128)(2,1)}, u32[]{:S(2)}, u32[]{:S(2)}) async-start(bf16[8,2,16384]{2,1,0:T(2,128)(2,1)} %reshape.354), calls=%async_computation.1 | async-start | bytes 1048576 | tf_op jit(solution)/shard_map/all_to_all | solution.py:42
  135.5 4.6 %copy-start.3 = (bf16[2,2,1,256,128]{4,2,3,0,1:T(2,128)(2,1)S(1)}, bf16[2,2,1,256,128]{4,2,3,0,1:T(2,128)(2,1)}, u32[]{:S(2)}) copy-start(bf16[2,2,1,256,128]{4,2,3,0,1:T(2,128)(2,1)} %get-tuple-element.304) | copy-start | bytes 786436
  135.5 4.6 %copy-start.4 = (bf16[2,2,1,256,128]{4,2,3,0,1:T(2,128)(2,1)S(1)}, bf16[2,2,1,256,128]{4,2,3,0,1:T(2,128)(2,1)}, u32[]{:S(2)}) copy-start(bf16[2,2,1,256,128]{4,2,3,0,1:T(2,128)(2,1)} %get-tuple-element.305) | copy-start | bytes 786436
  135.5 43.3 %collective-permute-start.1 = (bf16[4,2,2,256,128]{4,3,2,1,0:T(8,128)(2,1)}, bf16[4,2,2,256,128]{4,3,2,1,0:T(8,128)(2,1)}, u32[]{:S(2)}, u32[]{:S(2)}) collective-permute-start(bf16[4,2,2,256,128]{4,3,2,1,0:T(8,128)(2,1)} %bitcast.78), channel_id=1, source_target_pairs={{0,8},{8,0},{1,9},{9,1},{2,10},{10,2},{3,11},{11,3},{4,12},{12,4},... | collective-permute-start | bytes 3145736 | tf_op jit(solution)/shard_map/ppermute | solution.py:13
  180.7 1.2 copy-start.7
  180.7 1.2 copy-start.8
  181.9 1.0 copy-start.9
  181.9 1.0 copy-start.10
  186.7 3.2 copy-start.2
  189.9 2.0 copy-start.6
  191.9 1.1 copy-start.16
  196.7 2.0 copy-start.6
  198.7 1.1 copy-start.16
  203.5 2.0 copy-start.6
  205.5 1.1 copy-start.16
  210.3 2.0 copy-start.6
  212.3 1.1 copy-start.16
  217.2 5.8 %copy-start.11 = (bf16[4,256,128]{2,1,0:T(8,128)(2,1)}, bf16[4,256,128]{2,1,0:T(8,128)(2,1)S(1)}, u32[]{:S(2)}) copy-start(bf16[4,256,128]{2,1,0:T(8,128)(2,1)S(1)} %get-tuple-element.105) | copy-start | bytes 786436
  224.5 1.2 copy-start.1
  227.2 3.2 copy-start.15
  230.5 2.0 copy-start.5
  236.8 2.0 copy-start.5
  243.0 2.0 copy-start.5
  249.1 2.0 copy-start.5
  256.7 3.5 copy-start
  260.6 31.7 %collective-permute-start.3 = (bf16[20,256,128]{2,1,0:T(8,128)(2,1)S(1)}, bf16[20,256,128]{2,1,0:T(8,128)(2,1)S(1)}, u32[]{:S(2)}, u32[]{:S(2)}) collective-permute-start(bf16[20,256,128]{2,1,0:T(8,128)(2,1)S(1)} %pad_maximum_fusion.6), channel_id=1, source_target_pairs={{0,8},{8,0},{1,9},{9,1},{2,10},{10,2},{3,11},{11,3},{4,12},{12,4},... | collective-permute-start | bytes 3932168 | tf_op jit(solution)/shard_map/ppermute | solution.py:13
  261.3 57.6 %collective-permute-start.2 = (bf16[20,256,128]{2,1,0:T(8,128)(2,1)S(1)}, bf16[20,256,128]{2,1,0:T(8,128)(2,1)S(1)}, u32[]{:S(2)}, u32[]{:S(2)}) collective-permute-start(bf16[20,256,128]{2,1,0:T(8,128)(2,1)S(1)} %pad_maximum_fusion.5), channel_id=1, source_target_pairs={{0,8},{8,0},{1,9},{9,1},{2,10},{10,2},{3,11},{11,3},{4,12},{12,4},... | collective-permute-start | bytes 3932168 | tf_op jit(solution)/shard_map/ppermute | solution.py:13
  330.0 13.2 %copy-start.12 = (bf16[4,256,128]{2,1,0:T(8,128)(2,1)S(1)}, bf16[4,256,128]{2,1,0:T(8,128)(2,1)}, u32[]{:S(2)}) copy-start(bf16[4,256,128]{2,1,0:T(8,128)(2,1)} %copy-done.11) | copy-start | bytes 786436
  330.0 111.2 %all-to-all-start.3 = ((bf16[16,2,2,256,128]{4,3,1,2,0:T(8,128)(2,1)}), bf16[16,2,2,256,128]{4,3,1,2,0:T(8,128)(2,1)}, u32[]{:S(2)}, u32[]{:S(2)}) async-start(bf16[16,2,2,256,128]{4,3,1,2,0:T(8,128)(2,1)} %copy.346), calls=%async_computation.3 | async-start | bytes 8388608 | tf_op jit(solution)/shard_map/all_to_all | solution.py:180
  348.1 93.1 %copy-start.18 = (pred[16,2,4]{0,2,1:T(4,128)(4,1)S(1)}, pred[16,2,4]{0,2,1:T(4,128)(4,1)}, u32[]{:S(2)}) copy-start(pred[16,2,4]{0,2,1:T(4,128)(4,1)} %copy-done.17) | copy-start | bytes 388
